TPU v7x, 32 devices: a whole 2x2x4 slice. The times are simulated.
32 devices in a mesh: bucket: 8 (over z, x), rel: 4 (over y, core).
Axes of the slice: x: 2, y: 2, z: 4, core: 2. Of those that a mesh axis runs over, the one named last changes fastest.
Arguments:
- left_rows: float32 [8192, 512], P(('bucket', 'rel')), may hold values from -1.2 to 1.2
- left_state: float32 [8192], P(('bucket', 'rel')), may hold values from 1e-06 to 0.0001
- right_rows: float32 [8192, 512], P(('bucket', 'rel')), may hold values from -1.2 to 1.2
- right_state: float32 [8192], P(('bucket', 'rel')), may hold values from 1e-06 to 0.0001
- relations: bfloat16 [4, 512, 512], P('rel'), may hold values from -0.25 to 0.25
- fetch_ids: int32 [8, 4, 4], P('bucket', 'rel'), may hold values from 0 to 3
- edge_left: int32 [8, 4, 2, 512], P('bucket', 'rel'), may hold values from 0 to 255
- edge_right: int32 [8, 4, 2, 512], P('bucket', 'rel'), may hold values from 0 to 255
- edge_slot: int32 [8, 4, 2, 512], P('bucket', 'rel'), may hold values from 0 to 1
- edge_weight: int32 [8, 4, 2, 512], P('bucket', 'rel'), may hold values from 1 to 4
- matching: int32 [1], replicated, may hold values from 1 to 7
Outputs:
- left_out: float32 [8192, 512], P(('bucket', 'rel'))
- left_state_out: float32 [8192], P(('bucket', 'rel'))
- right_out: float32 [8192, 512], P(('bucket', 'rel'))
- right_state_out: float32 [8192], P(('bucket', 'rel'))
- rel_grad: float32 [4, 512, 512], P('rel')
Inputs may be any that keep to these rules, and one draw needn't show every extreme that they name: Bucket b is paired with bucket b XOR matching.
All inputs are finite; a program needn't handle non-finite values.
Results may differ from a plain program's by a relative error of at most 0.0015.
The roundings to bfloat16 on the way count: a program that leaves them out, or rounds other values in their place, can miss the bound.
Values may be sent and summed in bfloat16 or wider, within the bound.
No kernel may reach another device: no remote copies, remote signals or barrier semaphores. Data moves between devices by JAX's collectives and lax.ppermute only.
A program may use at most 64 MiB of HBM per device.

v0:
```python
import jax
import jax.numpy as jnp
from jax import lax
from jax.sharding import PartitionSpec as P

learn_rate = 0.1


def edge_targets(edge_left, edge_right, edge_slot, edge_weight, block_len):
    table = jnp.zeros((2, block_len, block_len), jnp.float32)
    table = table.at[edge_slot, edge_left, edge_right].add(edge_weight.astype(jnp.float32))
    return [table[0], table[1]]


def adagrad(table, state, gradient):
    state_new = state + jnp.mean(gradient * gradient, axis=1)
    return (table - learn_rate * gradient / jnp.sqrt(state_new)[:, None], state_new)


def one_round(
    left_block,
    left_st,
    right_block,
    right_st,
    rel_pair,
    edge_left,
    edge_right,
    edge_slot,
    edge_weight,
):
    block_len = left_block.shape[0]
    left_half = left_block.astype(jnp.bfloat16)
    right_half = right_block.astype(jnp.bfloat16)
    targets = edge_targets(edge_left, edge_right, edge_slot, edge_weight, block_len)
    grad_left = jnp.zeros(left_block.shape, jnp.float32)
    grad_right = jnp.zeros(right_block.shape, jnp.float32)
    rel_grads = []
    for slot_index in range(2):
        matrix = rel_pair[slot_index]
        projected = jnp.dot(left_half, matrix, preferred_element_type=jnp.float32).astype(
            jnp.bfloat16
        )
        scores = jnp.dot(projected, right_half.T, preferred_element_type=jnp.float32)
        score_grad = ((jax.nn.sigmoid(scores) - targets[slot_index]) / block_len).astype(
            jnp.bfloat16
        )
        carried = jnp.dot(score_grad, right_half, preferred_element_type=jnp.float32).astype(
            jnp.bfloat16
        )
        grad_left = grad_left + jnp.dot(carried, matrix.T, preferred_element_type=jnp.float32)
        grad_right = grad_right + jnp.dot(
            score_grad.T, projected, preferred_element_type=jnp.float32
        )
        rel_grads.append(jnp.dot(left_half.T, carried, preferred_element_type=jnp.float32))
    left_new, left_st_new = adagrad(left_block, left_st, grad_left)
    right_new, right_st_new = adagrad(right_block, right_st, grad_right)
    return (left_new, left_st_new, right_new, right_st_new, rel_grads)


def partner_blocks(row_block, state_block, switch):
    block_len = row_block.shape[0]
    width = row_block.shape[1]
    partner = jnp.bitwise_xor(lax.axis_index("bucket"), switch)
    portion = (
        lax.all_gather(row_block, "bucket", axis=0, tiled=True),
        lax.all_gather(state_block, "bucket", axis=0, tiled=True),
    )
    block_count = portion[0].shape[0] // block_len
    owners = jnp.arange(block_count, dtype=jnp.int32)
    chosen = owners == partner
    rows_part = portion[0].reshape(block_count, block_len, width)
    states_part = portion[1].reshape(block_count, block_len)
    rows_new = jnp.sum(jnp.where(chosen[:, None, None], rows_part, jnp.float32(0.0)), axis=0)
    states_new = jnp.sum(jnp.where(chosen[:, None], states_part, jnp.float32(0.0)), axis=0)
    return (rows_new, states_new)


def reduce_gradients(gradients, rel_ids, rel_total, width):
    stacked = jnp.stack(gradients)
    own_rows = rel_total // lax.axis_size("rel") * width
    rel_count_piece = own_rows * lax.axis_size("rel") // width
    rel_list = jnp.arange(rel_count_piece, dtype=jnp.int32)
    weights = (rel_ids[:, None] == rel_list[None, :]).astype(jnp.float32)
    term = jnp.einsum("sk,sde->kde", weights, stacked, precision=lax.Precision.HIGHEST)
    partial_sum = lax.psum_scatter(
        term.reshape(rel_count_piece * width, width), "rel", scatter_dimension=0, tiled=True
    )
    return lax.psum(partial_sum, "bucket")


def on_device(
    left_rows,
    left_state,
    right_rows,
    right_state,
    relations,
    fetch_ids,
    edge_left,
    edge_right,
    edge_slot,
    edge_weight,
    matching,
):
    width = relations.shape[1]
    rel_table = lax.all_gather(relations, "rel", axis=0, tiled=True)
    rel_total = rel_table.shape[0]
    rel_ids = fetch_ids[0, 0]
    switch = matching[0]
    table_left, state_left = (left_rows, left_state)
    row_block, state_block = (right_rows, right_state)
    gradients = []
    for round_index in range(2):
        rel_pair = jnp.take(rel_table, rel_ids[2 * round_index : 2 * round_index + 2], axis=0)
        table_left, state_left, row_block, state_block, rel_grads = one_round(
            table_left,
            state_left,
            row_block,
            state_block,
            rel_pair,
            edge_left[0, 0, round_index],
            edge_right[0, 0, round_index],
            edge_slot[0, 0, round_index],
            edge_weight[0, 0, round_index],
        )
        gradients.extend(rel_grads)
        if round_index == 0:
            row_block, state_block = partner_blocks(row_block, state_block, switch)
    owned = reduce_gradients(gradients, rel_ids, rel_total, width)
    return (table_left, state_left, row_block, state_block, owned.reshape(-1, width, width))


def solution(mesh):
    in_specs = (
        P(("bucket", "rel"), None),
        P(("bucket", "rel")),
        P(("bucket", "rel"), None),
        P(("bucket", "rel")),
        P("rel", None, None),
        P("bucket", "rel", None),
        P("bucket", "rel", None, None),
        P("bucket", "rel", None, None),
        P("bucket", "rel", None, None),
        P("bucket", "rel", None, None),
        P(),
    )
    out_specs = (
        P(("bucket", "rel"), None),
        P(("bucket", "rel")),
        P(("bucket", "rel"), None),
        P(("bucket", "rel")),
        P("rel", None, None),
    )
    return jax.shard_map(
        on_device, mesh=mesh, in_specs=in_specs, out_specs=out_specs, check_vma=False
    )
```

profile of v0, /device:TPU:0, one launch (start us, length us, event | category | flops | bytes accessed | tf_op | source)
XLA Modules:
  0.0 281.4 jit_solution(3566939604815437510)
XLA Ops:
  7.2 0.7 all-gather.4.cloned.1.call-update
  8.0 1.1 convert_element_type.65
  9.0 1.1 convert_element_type.63
  10.1 0.8 slice_convert_fusion
  10.9 0.8 or_select_fusion
  11.7 31.3 %scatter_fusion = f32[2,256,256]{2,1,0:T(8,128)S(1)} fusion(f32[2,256,256]{2,1,0:T(8,128)S(1)} %broadcast.145.clone, s32[512]{0:T(512)S(1)} %bitcast.126, f32[512]{0:T(512)S(1)} %bitcast.131), kind=kCustom, calls=%fused_computation.2 | custom fusion | flops 512 | bytes 12288 | tf_op jit(solution)/shard_map/scatter-add | solution.py:11
  43.1 0.6 compare_and_fusion
  43.7 2.2 gather_fusion
  48.6 0.9 divide_subtract_fusion.2
  50.5 31.3 %scatter_fusion.1 = f32[2,256,256]{2,1,0:T(8,128)S(1)} fusion(f32[2,256,256]{2,1,0:T(8,128)S(1)} %broadcast.145.clone.1, s32[512]{0:T(512)S(1)} %bitcast.125, f32[512]{0:T(512)S(1)} %bitcast.130), kind=kCustom, calls=%fused_computation.3 | custom fusion | flops 512 | bytes 12288 | tf_op jit(solution)/shard_map/scatter-add | solution.py:11
  82.3 3.2 %gather_fusion.1 = bf16[2,512,512]{2,1,0:T(8,128)(2,1)} fusion(bf16[4,512,512]{2,1,0:T(8,128)(2,1)} %all-gather.4.cloned.1.call-done, s32[1024]{0:T(1024)S(1)} %get-tuple-element.30), kind=kCustom, calls=%fused_computation.1.clone | custom fusion | bytes 2097160 | tf_op jit(solution)/shard_map/jit(_take)/gather | solution.py:113
  85.8 1.3 convolution_bitcast_fusion.2
  87.3 1.3 convolution_bitcast_fusion.3
  90.0 1.0 convolution_convert_fusion.3
  91.1 34.1 %all-gather.6.cloned.1.call-done = f32[2048,512]{1,0:T(8,128)} async-done(((f32[256,512]{1,0:T(8,128)}), f32[2048,512]{1,0:T(8,128)}) %all-gather.6.cloned.1.call-update) | async-done | bytes 4194320 | tf_op jit(solution)/shard_map/all_gather | solution.py:65
  125.2 2.9 %select_reduce_fusion = f32[256,512]{1,0:T(8,128)S(1)} fusion(f32[8,256,512]{2,1,0:T(8,128)} %bitcast.128, pred[8]{0:T(512)(128)(4,1)S(1)} %copy-done.14), kind=kLoop, calls=%fused_computation.5 | loop fusion | flops 1966080 | bytes 4718600 | tf_op jit(solution)/shard_map/reduce_sum | solution.py:73
  130.3 2.4 pad_maximum_fusion
  132.7 5.5 %copy.25 = f32[4,512,512]{2,0,1:T(4,128)} copy(f32[4,512,512]{1,2,0:T(8,128)} %pad_maximum_fusion) | data formatting | bytes 8388608 | tf_op jit(solution)/shard_map/stack | solution.py:79
  138.2 6.2 %fusion.32 = f32[4,512,512]{2,0,1:T(4,128)S(1)} fusion(f32[4,512,512]{2,0,1:T(4,128)} %copy.25, s32[4]{0:T(128)S(1)} %bitcast.132), kind=kOutput, calls=%fused_computation.98 | convolution fusion | flops 50331664 | bytes 8388624 | tf_op jit(solution)/shard_map/sk,sde->kde/dot_general | solution.py:84
  144.4 3.2 %copy.26 = f32[4,512,512]{2,1,0:T(8,128)} copy(f32[4,512,512]{2,0,1:T(4,128)S(1)} %fusion.32) | data formatting | bytes 8388608 | tf_op jit(solution)/shard_map/sk,sde->kde/dot_general | solution.py:84
  147.7 0.6 copy-done.13
  148.3 18.1 %all-gather = f32[8,1,256]{2,1,0:T(1,128)S(1)} all-gather(f32[1,1,256]{2,1,0:T(1,128)S(1)} %bitcast.133), channel_id=1, replica_groups=mesh['bucket'=8,'rel'=4] {'bucket'}, dimensions={0}, use_global_device_ids=true | all-gather | bytes 9216 | tf_op jit(solution)/shard_map/all_gather | solution.py:66
  166.5 1.2 fusion.41
  167.7 1.1 fusion.25
  168.9 2.0 multiply_reduce_fusion
  170.9 20.1 %reduce-scatter.2.cloned.1.call-done = f32[512,512]{1,0:T(8,128)} async-done(((f32[2048,512]{1,0:T(8,128)}), f32[512,512]{1,0:T(8,128)}) %reduce-scatter.2.cloned.1.call-update) | async-done | bytes 1048592 | tf_op jit(solution)/shard_map/reduce_scatter | solution.py:85
  191.6 1.5 multiply_reduce_fusion.1
  193.0 0.6 fusion.38
  193.6 2.0 divide_subtract_fusion
  195.5 1.0 divide_subtract_fusion.1
  196.6 76.1 %all-reduce.2.cloned.1.call-done = f32[1,512,512]{2,1,0:T(8,128)} async-done(((f32[1,512,512]{2,1,0:T(8,128)}), f32[1,512,512]{2,1,0:T(8,128)}) %all-reduce.2.cloned.1.call-update) | async-done | bytes 1048592 | tf_op jit(solution)/shard_map/psum | solution.py:88
  272.6 2.3 copy.35
  (72 shorter events, 8.3 us)
Async XLA Ops:
  7.2 35.9 %copy-start.11 = (s32[1,1,4]{2,1,0:T(1,128)S(1)}, s32[1,1,4]{2,1,0:T(1,128)}, u32[]{:S(2)}) copy-start(s32[1,1,4]{2,1,0:T(1,128)} %param.18) | copy-start | bytes 52
  7.2 36.5 %all-gather.4.cloned.1.call-start = ((), (), s32[]{:S(2)}) async-start(), calls=%async_computation.1 | async-start | bytes 2621440 | tf_op jit(solution)/shard_map/all_gather | solution.py:105
  7.9 117.3 %all-gather.6.cloned.1.call-start = ((), (), s32[]{:S(2)}) async-start(), calls=%async_computation.2 | async-start | bytes 4718592 | tf_op jit(solution)/shard_map/all_gather | solution.py:65
  46.1 2.0 copy-start.17
  46.1 2.5 copy-start.6
  49.6 141.4 %reduce-scatter.2.cloned.1.call-start = ((), (), s32[]{:S(2)}) async-start(), calls=%async_computation.3 | async-start | bytes 5242880 | tf_op jit(solution)/shard_map/reduce_scatter | solution.py:85
  85.5 3.9 %copy-start.12 = (f32[256]{0:T(256)S(1)}, f32[256]{0:T(256)}, u32[]{:S(2)}) copy-start(f32[256]{0:T(256)} %param.14) | copy-start | bytes 3076
  85.5 3.9 %copy-start = (f32[256,512]{1,0:T(8,128)S(1)}, f32[256,512]{1,0:T(8,128)}, u32[]{:S(2)}) copy-start(f32[256,512]{1,0:T(8,128)} %param.13) | copy-start | bytes 1572868
  85.7 3.8 %copy-start.1 = (bf16[2,512,512]{2,1,0:T(8,128)(2,1)S(1)}, bf16[2,512,512]{2,1,0:T(8,128)(2,1)}, u32[]{:S(2)}) copy-start(bf16[2,512,512]{2,1,0:T(8,128)(2,1)} %gather_fusion.1) | copy-start | bytes 3145732
  85.8 3.8 %copy-start.16 = (pred[2]{0:T(512)(128)(4,1)S(1)}, pred[2]{0:T(512)(128)(4,1)}, u32[]{:S(2)}) copy-start(pred[2]{0:T(512)(128)(4,1)} %get-tuple-element.12) | copy-start | bytes 10
  88.6 36.6 %copy-start.14 = (pred[8]{0:T(512)(128)(4,1)S(1)}, pred[8]{0:T(512)(128)(4,1)}, u32[]{:S(2)}) copy-start(pred[8]{0:T(512)(128)(4,1)} %iota_compare_fusion.1) | copy-start | bytes 28
  89.5 35.7 %copy-start.4 = (bf16[256,512]{1,0:T(8,128)(2,1)}, bf16[256,512]{1,0:T(8,128)(2,1)S(1)}, u32[]{:S(2)}) copy-start(bf16[256,512]{1,0:T(8,128)(2,1)S(1)} %fusion.36) | copy-start | bytes 786436
  90.0 38.1 %copy-start.9 = (bf16[256,512]{1,0:T(8,128)(2,1)}, bf16[256,512]{1,0:T(8,128)(2,1)S(1)}, u32[]{:S(2)}) copy-start(bf16[256,512]{1,0:T(8,128)(2,1)S(1)} %convolution_convert_fusion.1) | copy-start | bytes 786436
  125.2 3.5 %copy-start.10 = (bf16[256,512]{1,0:T(8,128)(2,1)S(1)}, bf16[256,512]{1,0:T(8,128)(2,1)}, u32[]{:S(2)}) copy-start(bf16[256,512]{1,0:T(8,128)(2,1)} %convolution_convert_fusion.3) | copy-start | bytes 786436
  125.2 4.4 %copy-start.5 = (bf16[256,512]{1,0:T(8,128)(2,1)S(1)}, bf16[256,512]{1,0:T(8,128)(2,1)}, u32[]{:S(2)}) copy-start(bf16[256,512]{1,0:T(8,128)(2,1)} %copy-done.4) | copy-start | bytes 786436
  128.1 2.3 copy-start.2
  128.1 2.3 copy-start.3
  129.0 0.7 copy-start.7
  147.7 0.7 copy-start.13
  147.7 18.8 %copy-start.15 = (pred[8]{0:T(512)(128)(4,1)S(1)}, pred[8]{0:T(512)(128)(4,1)}, u32[]{:S(2)}) copy-start(pred[8]{0:T(512)(128)(4,1)} %iota_compare_fusion.1) | copy-start | bytes 28
  147.7 18.9 %copy-start.8 = (bf16[256,256]{1,0:T(8,128)(2,1)S(1)}, bf16[256,256]{1,0:T(8,128)(2,1)}, u32[]{:S(2)}) copy-start(bf16[256,256]{1,0:T(8,128)(2,1)} %copy-done.7) | copy-start | bytes 393220
  147.7 124.9 %all-reduce.2.cloned.1.call-start = ((), (), s32[]{:S(2)}) async-start(), calls=%async_computation.4 | async-start | bytes 2097152 | tf_op jit(solution)/shard_map/psum | solution.py:88
Sparse Core Ops, SparseCore 0:
  9.5 25.2 all-gather.3
  49.7 75.4 all-gather.5
  147.8 43.1 reduce-scatter.1
  194.3 78.2 all-reduce.1
where the time goes:
time: 282 us; the launch traced here: 281 us
  waiting for transfers between devices  131 us (46%)
  other arithmetic  79 us (28%)
  matrix products  20.7 us (7%)
  blocking collectives  18.1 us (6%)
  local copies, waits for them, and re-layouts  17.5 us (6%)
  between operations  14.8 us (5%)
    psum x1, waiting for transfers between devices, reduce_gradients(): return lax.psum(partial_sum, 'bucket')  76.1 us
    scatter-add x2, other arithmetic, edge_targets(): table.at[edge_slot, edge_left, edge_right]  62.7 us
    all_gather x1, waiting for transfers between devices, partner_blocks(): lax.all_gather(row_block, 'bucket', axis=0, tiled=True)  34.1 us
    reduce_scatter x1, waiting for transfers between devices, reduce_gradients(): lax.psum_scatter(term.reshape(rel_count_piece * width, width), 'rel', sca...  20.1 us
    all_gather x1, blocking collectives, partner_blocks(): lax.all_gather(state_block, 'bucket', axis=0, tiled=True)  18.1 us
    dot_general x1, matrix products, reduce_gradients(): jnp.einsum('sk,sde->kde', weights, stacked, precision=lax.Precision.HIGHEST)  6.2 us
  transfers between devices with their start and end apart: 4, of which 3 were waited for; matrix products, arithmetic and copies ran while one was open for 31% of the time, Pallas kernels for 0%

commit v1 on v0

--- a/solution.py
+++ b/solution.py
@@ -62,7 +62,9 @@
     width = row_block.shape[1]
     partner = jnp.bitwise_xor(lax.axis_index("bucket"), switch)
     portion = (
-        lax.all_gather(row_block, "bucket", axis=0, tiled=True),
+        jnp.concatenate(
+            lax.all_to_all(jnp.stack([row_block] * lax.axis_size("bucket")), "bucket", 0, 0), axis=0
+        ),
         lax.all_gather(state_block, "bucket", axis=0, tiled=True),
     )
     block_count = portion[0].shape[0] // block_len

time: 282 us -> 309 us (1.096)
  waiting for transfers between devices: 131 us -> 149 us
  starting transfers between devices: 0.34 us -> 7.53 us
    all_to_all x0 -> x1, waiting for transfers between devices: none -> 51.7 us  [partner_blocks(): lax.all_to_all(jnp.stack([row_block] * lax.axis_size('bucket')), 'bucket'...]
    all_gather x1 -> x0, waiting for transfers between devices: 34.1 us -> none  [partner_blocks(): lax.all_gather(row_block, 'bucket', axis=0, tiled=True)]
    all_to_all x0 -> x1, starting transfers between devices: none -> 7.23 us  [partner_blocks(): lax.all_to_all(jnp.stack([row_block] * lax.axis_size('bucket')), 'bucket'...]
  transfers between devices with their start and end apart: 4 -> 4, of which waited for: 3 -> 3; matrix products, arithmetic and copies ran while one was open for 31% -> 28% of each run, Pallas kernels for 0% -> 0%
where the time goes in v1:
time: 309 us; the launch traced here: 308 us
  waiting for transfers between devices  149 us (48%)
  other arithmetic  78.4 us (25%)
  matrix products  20 us (6%)
  local copies, waits for them, and re-layouts  19.6 us (6%)
  blocking collectives  18.6 us (6%)
  between operations  14.8 us (5%)
  starting transfers between devices  7.53 us (2%)
    psum x1, waiting for transfers between devices, reduce_gradients(): return lax.psum(partial_sum, 'bucket')  76.5 us
    scatter-add x2, other arithmetic, edge_targets(): table.at[edge_slot, edge_left, edge_right]  62.7 us
    all_to_all x1, waiting for transfers between devices, partner_blocks(): lax.all_to_all(jnp.stack([row_block] * lax.axis_size('bucket')), 'bucket'...  51.7 us
    reduce_scatter x1, waiting for transfers between devices, reduce_gradients(): lax.psum_scatter(term.reshape(rel_count_piece * width, width), 'rel', sca...  20.2 us
    all_gather x1, blocking collectives, partner_blocks(): lax.all_gather(state_block, 'bucket', axis=0, tiled=True)  18.6 us
    all_to_all x1, starting transfers between devices, partner_blocks(): lax.all_to_all(jnp.stack([row_block] * lax.axis_size('bucket')), 'bucket'...  7.23 us
    dot_general x1, matrix products, reduce_gradients(): jnp.einsum('sk,sde->kde', weights, stacked, precision=lax.Precision.HIGHEST)  6.2 us
  transfers between devices with their start and end apart: 4, of which 3 were waited for; matrix products, arithmetic and copies ran while one was open for 28% of the time, Pallas kernels for 0%

profile of v1, /device:TPU:0, one launch (start us, length us, event | category | flops | bytes accessed | tf_op | source)
XLA Modules:
  0.0 308.2 jit_solution(6568396244047299165)
XLA Ops:
  7.2 0.7 all-gather.3.cloned.1.call-update
  7.9 1.1 convert_element_type.63
  9.0 1.1 convert_element_type.65
  10.1 0.8 slice_convert_fusion
  10.8 0.8 or_select_fusion
  11.7 31.3 %scatter_fusion = f32[2,256,256]{2,1,0:T(8,128)S(1)} fusion(f32[2,256,256]{2,1,0:T(8,128)S(1)} %broadcast.147.clone, s32[512]{0:T(512)S(1)} %bitcast.125, f32[512]{0:T(512)S(1)} %bitcast.129), kind=kCustom, calls=%fused_computation.2 | custom fusion | flops 512 | bytes 12288 | tf_op jit(solution)/shard_map/scatter-add | solution.py:11
  43.6 2.2 gather_fusion
  48.7 2.5 stack.12
  51.2 7.2 %all-to-all-start = ((f32[8,256,512]{2,1,0:T(8,128)}), f32[8,256,512]{2,1,0:T(8,128)}, u32[]{:S(2)}, u32[]{:S(2)}) async-start(f32[8,256,512]{2,1,0:T(8,128)} %stack.12), calls=%async_computation | async-start | bytes 8388608 | tf_op jit(solution)/shard_map/all_to_all | solution.py:66
  59.4 31.3 %scatter_fusion.1 = f32[2,256,256]{2,1,0:T(8,128)S(1)} fusion(f32[2,256,256]{2,1,0:T(8,128)S(1)} %broadcast.147.clone.1, s32[512]{0:T(512)S(1)} %bitcast.124, f32[512]{0:T(512)S(1)} %bitcast.128), kind=kCustom, calls=%fused_computation.3 | custom fusion | flops 512 | bytes 12288 | tf_op jit(solution)/shard_map/scatter-add | solution.py:11
  91.3 3.2 %gather_fusion.1 = bf16[2,512,512]{2,1,0:T(8,128)(2,1)} fusion(bf16[4,512,512]{2,1,0:T(8,128)(2,1)} %all-gather.3.cloned.1.call-done, s32[1024]{0:T(1024)S(1)} %get-tuple-element.30), kind=kCustom, calls=%fused_computation.1.clone | custom fusion | bytes 2097160 | tf_op jit(solution)/shard_map/jit(_take)/gather | solution.py:115
  94.7 1.4 convolution_bitcast_fusion.2
  96.3 1.3 convolution_bitcast_fusion.3
  99.0 1.0 convolution_convert_fusion.1
  100.0 51.7 %all-to-all-done = f32[8,256,512]{2,1,0:T(8,128)} async-done(((f32[8,256,512]{2,1,0:T(8,128)}), f32[8,256,512]{2,1,0:T(8,128)}, u32[]{:S(2)}, u32[]{:S(2)}) %all-to-all-start) | async-done | bytes 4194336 | tf_op jit(solution)/shard_map/all_to_all | solution.py:66
  151.8 2.9 select_reduce_fusion
  156.5 2.4 pad_maximum_fusion
  158.9 5.5 %copy.29 = f32[4,512,512]{2,0,1:T(4,128)} copy(f32[4,512,512]{1,2,0:T(8,128)} %pad_maximum_fusion) | data formatting | bytes 8388608 | tf_op jit(solution)/shard_map/stack | solution.py:81
  164.4 6.2 %fusion.32 = f32[4,512,512]{2,0,1:T(4,128)S(1)} fusion(f32[4,512,512]{2,0,1:T(4,128)} %copy.29, s32[4]{0:T(128)S(1)} %bitcast.130), kind=kOutput, calls=%fused_computation.98 | convolution fusion | flops 50331664 | bytes 8388624 | tf_op jit(solution)/shard_map/sk,sde->kde/dot_general | solution.py:86
  170.6 3.2 %copy.30 = f32[4,512,512]{2,1,0:T(8,128)} copy(f32[4,512,512]{2,0,1:T(4,128)S(1)} %fusion.32) | data formatting | bytes 8388608 | tf_op jit(solution)/shard_map/sk,sde->kde/dot_general | solution.py:86
  174.5 18.6 %all-gather = f32[8,1,256]{2,1,0:T(1,128)S(1)} all-gather(f32[1,1,256]{2,1,0:T(1,128)S(1)} %bitcast.131), channel_id=1, replica_groups=mesh['bucket'=8,'rel'=4] {'bucket'}, dimensions={0}, use_global_device_ids=true | all-gather | bytes 9216 | tf_op jit(solution)/shard_map/all_gather | solution.py:68
  193.1 0.6 fusion.26
  193.8 1.2 fusion.41
  195.0 1.1 fusion.25
  196.1 1.3 multiply_reduce_fusion
  197.4 20.2 %reduce-scatter.2.cloned.1.call-done = f32[512,512]{1,0:T(8,128)} async-done(((f32[2048,512]{1,0:T(8,128)}), f32[512,512]{1,0:T(8,128)}) %reduce-scatter.2.cloned.1.call-update) | async-done | bytes 1048592 | tf_op jit(solution)/shard_map/reduce_scatter | solution.py:87
  217.6 1.2 fusion.37
  218.9 1.5 multiply_reduce_fusion.1
  220.9 0.9 divide_subtract_fusion
  221.8 1.0 divide_subtract_fusion.1
  222.8 76.5 %all-reduce.2.cloned.1.call-done = f32[1,512,512]{2,1,0:T(8,128)} async-done(((f32[1,512,512]{2,1,0:T(8,128)}), f32[1,512,512]{2,1,0:T(8,128)}) %all-reduce.2.cloned.1.call-update) | async-done | bytes 1048592 | tf_op jit(solution)/shard_map/psum | solution.py:90
  299.4 2.3 copy.39
  (72 shorter events, 9.2 us)
Async XLA Ops:
  7.2 35.9 %copy-start.11 = (s32[1,1,4]{2,1,0:T(1,128)S(1)}, s32[1,1,4]{2,1,0:T(1,128)}, u32[]{:S(2)}) copy-start(s32[1,1,4]{2,1,0:T(1,128)} %param.18) | copy-start | bytes 52
  7.2 36.5 %all-gather.3.cloned.1.call-start = ((), (), s32[]{:S(2)}) async-start(), calls=%async_computation.2 | async-start | bytes 2621440 | tf_op jit(solution)/shard_map/all_gather | solution.py:107
  46.0 2.0 copy-start.17
  46.0 2.5 copy-start.6
  51.2 100.5 %all-to-all-start = ((f32[8,256,512]{2,1,0:T(8,128)}), f32[8,256,512]{2,1,0:T(8,128)}, u32[]{:S(2)}, u32[]{:S(2)}) async-start(f32[8,256,512]{2,1,0:T(8,128)} %stack.12), calls=%async_computation | async-start | bytes 8388608 | tf_op jit(solution)/shard_map/all_to_all | solution.py:66
  58.4 159.2 %reduce-scatter.2.cloned.1.call-start = ((), (), s32[]{:S(2)}) async-start(), calls=%async_computation.3 | async-start | bytes 5242880 | tf_op jit(solution)/shard_map/reduce_scatter | solution.py:87
  94.4 3.9 %copy-start.12 = (f32[256]{0:T(256)S(1)}, f32[256]{0:T(256)}, u32[]{:S(2)}) copy-start(f32[256]{0:T(256)} %param.14) | copy-start | bytes 3076
  94.4 3.9 %copy-start = (f32[256,512]{1,0:T(8,128)S(1)}, f32[256,512]{1,0:T(8,128)}, u32[]{:S(2)}) copy-start(f32[256,512]{1,0:T(8,128)} %param.13) | copy-start | bytes 1572868
  94.7 3.9 %copy-start.1 = (bf16[2,512,512]{2,1,0:T(8,128)(2,1)S(1)}, bf16[2,512,512]{2,1,0:T(8,128)(2,1)}, u32[]{:S(2)}) copy-start(bf16[2,512,512]{2,1,0:T(8,128)(2,1)} %gather_fusion.1) | copy-start | bytes 3145732
  94.7 3.9 %copy-start.16 = (pred[2]{0:T(512)(128)(4,1)S(1)}, pred[2]{0:T(512)(128)(4,1)}, u32[]{:S(2)}) copy-start(pred[2]{0:T(512)(128)(4,1)} %get-tuple-element.12) | copy-start | bytes 10
  97.6 54.1 %copy-start.14 = (pred[8]{0:T(512)(128)(4,1)S(1)}, pred[8]{0:T(512)(128)(4,1)}, u32[]{:S(2)}) copy-start(pred[8]{0:T(512)(128)(4,1)} %iota_compare_fusion.1) | copy-start | bytes 28
  98.5 1.5 copy-start.4
  99.0 55.7 %copy-start.10 = (bf16[256,512]{1,0:T(8,128)(2,1)}, bf16[256,512]{1,0:T(8,128)(2,1)S(1)}, u32[]{:S(2)}) copy-start(bf16[256,512]{1,0:T(8,128)(2,1)S(1)} %convolution_convert_fusion.3) | copy-start | bytes 786436
  151.7 3.5 %copy-start.9 = (bf16[256,512]{1,0:T(8,128)(2,1)S(1)}, bf16[256,512]{1,0:T(8,128)(2,1)}, u32[]{:S(2)}) copy-start(bf16[256,512]{1,0:T(8,128)(2,1)} %convolution_convert_fusion.1) | copy-start | bytes 786436
  151.8 4.0 %copy-start.5 = (bf16[256,512]{1,0:T(8,128)(2,1)S(1)}, bf16[256,512]{1,0:T(8,128)(2,1)}, u32[]{:S(2)}) copy-start(bf16[256,512]{1,0:T(8,128)(2,1)} %copy-done.4) | copy-start | bytes 786436
  154.6 1.9 copy-start.2
  154.6 1.9 copy-start.3
  155.0 0.8 copy-start.7
  173.8 0.7 copy-start.13
  173.8 19.3 %copy-start.15 = (pred[8]{0:T(512)(128)(4,1)S(1)}, pred[8]{0:T(512)(128)(4,1)}, u32[]{:S(2)}) copy-start(pred[8]{0:T(512)(128)(4,1)} %iota_compare_fusion.1) | copy-start | bytes 28
  173.8 19.9 %copy-start.8 = (bf16[256,256]{1,0:T(8,128)(2,1)S(1)}, bf16[256,256]{1,0:T(8,128)(2,1)}, u32[]{:S(2)}) copy-start(bf16[256,256]{1,0:T(8,128)(2,1)} %copy-done.7) | copy-start | bytes 393220
  173.9 125.5 %all-reduce.2.cloned.1.call-start = ((), (), s32[]{:S(2)}) async-start(), calls=%async_computation.4 | async-start | bytes 2097152 | tf_op jit(solution)/shard_map/psum | solution.py:90
Sparse Core Ops, SparseCore 0:
  9.5 25.2 all-gather.2
  174.0 43.5 reduce-scatter.1
  221.1 78.2 all-reduce.1
